TPU v7x, 32 devices: a whole 2x2x4 slice. The times are simulated.
32 devices in a mesh: groups: 2 (over x), wide: 4 (over y, core), expert: 4 (over z).
Axes of the slice: x: 2, y: 2, z: 4, core: 2. Of those that a mesh axis runs over, the one named last changes fastest.
Arguments:
- prompts: bfloat16 [8, 128, 6144], P(('groups', 'wide'), None, 'expert'), parts along dimension 0, may hold values from -6 to 6
- span_slot_owner: int32 [8], P('groups'), parts along dimension 0, may hold values from 0 to 3, as said below
- row_expert_index: int32 [768, 2], P('groups'), parts along dimension 0, may hold values from 0 to 7, all different within a row
- tile_tenant_index: int32 [6], P('groups'), parts along dimension 0, may hold values from 0 to 7
- tenant_adapter_slot: int32 [16], P('groups'), parts along dimension 0, may hold values from 0 to 7, each once
- router: bfloat16 [6144, 8], replicated, may hold values from -0.078125 to 0.078125
- gate_weight: bfloat16 [2, 6144, 16384], P(None, None, ('wide', 'expert')), may hold values from -0.078125 to 0.078125
- up_weight: bfloat16 [2, 6144, 16384], P(None, None, ('wide', 'expert')), may hold values from -0.078125 to 0.078125
- down_weight: bfloat16 [2, 16384, 6144], P(None, 'wide', 'expert'), may hold values from -0.046875 to 0.046875
- adapter_down_weight: bfloat16 [16, 2, 6144, 64], P(('groups', 'wide'), None, 'expert'), parts along dimension 0, may hold values from -0.078125 to 0.078125
- adapter_up_weight: bfloat16 [16, 2, 64, 16384], P('groups', None, None, ('wide', 'expert')), parts along dimension 0, may hold values from -0.75 to 0.75
Outputs:
- mixed: bfloat16 [768, 6144], P(('groups', 'wide'), 'expert'), parts along dimension 0
There are 2 independent parts, one for each index of `groups`. A program takes and returns all parts, laid end to end along the dimension named above; an argument that names none is the same for every part. Nothing has to cross between parts.
Inputs may be any that keep to these rules, and one draw needn't show every extreme that they name: `span_slot_owner`: a permutation of the slots; span c, for c < 3, is in slot span_slot_owner[c]. `row_expert_index`: each row names two different experts. `tenant_adapter_slot`: a permutation of the slots. `tile_tenant_index`: tenant of rows 128 * i to 128 * i + 127.
All inputs are finite; a program needn't handle non-finite values.
Results may differ from a plain program's by a relative error of at most 0.0051.
Values may be sent and summed in bfloat16 or wider, within the bound.
No kernel may reach another device: no remote copies, remote signals or barrier semaphores. Data moves between devices by JAX's collectives and lax.ppermute only.
A program may use at most 128 MiB of HBM per device.

v0:
```python
import jax
import jax.numpy as jnp
from jax import lax
from jax.sharding import PartitionSpec as P

NCHUNK = 3
ADAPTER_SCALE = 0.5


def spread(block, axis, source):
    block = jnp.where(lax.axis_index(axis) == source, block, jnp.zeros_like(block))
    return lax.psum(block, axis)


def per_device(
    prompts,
    span_slot_owner,
    row_expert_index,
    tile_tenant_index,
    tenant_adapter_slot,
    router,
    gate_weight,
    up_weight,
    down_weight,
    adapter_down_weight,
    adapter_up_weight,
):
    column = lax.axis_index("expert")
    own_slot = prompts[0]
    width_part = own_slot.shape[1]
    full_slot = lax.all_gather(own_slot, "expert", axis=1, tiled=True)
    pieces = [
        spread(full_slot, "wide", span_slot_owner[span_index]) for span_index in range(NCHUNK)
    ]
    input_rows = jnp.concatenate(pieces, axis=0)
    slices = lax.dynamic_slice_in_dim(input_rows, column * width_part, width_part, 1)
    tokens = input_rows.shape[0]
    window = gate_weight.shape[0]
    logits = jnp.dot(input_rows, router, preferred_element_type=jnp.float32)
    experts = jnp.arange(router.shape[1], dtype=jnp.int32)
    picked = (row_expert_index[:, :, None] == experts[None, None, :]).astype(jnp.float32)
    chosen = jnp.sum(picked * logits[:, None, :], axis=2)
    first_prob = jax.nn.sigmoid(chosen[:, 0] - chosen[:, 1])
    second_prob = jax.nn.sigmoid(chosen[:, 1] - chosen[:, 0])
    weight = (
        first_prob[:, None] * picked[:, 0, :window] + second_prob[:, None] * picked[:, 1, :window]
    )
    tile_count = tile_tenant_index.shape[0]
    tile_rows = tokens // tile_count
    resident_slots = adapter_down_weight.shape[0]
    tile_slot_index = jnp.take(tenant_adapter_slot, tile_tenant_index)
    owners = tile_slot_index // resident_slots
    local_expert_index = tile_slot_index % resident_slots
    tile_slices = slices.reshape(tile_count, tile_rows, width_part)

    def fetch_one(state_carry, tile_position):
        adapter_piece = lax.dynamic_index_in_dim(
            adapter_down_weight, local_expert_index[tile_position], 0, keepdims=False
        )
        return (state_carry, spread(adapter_piece, "wide", owners[tile_position]))

    unused, fetched = lax.scan(fetch_one, jnp.int32(0), jnp.arange(tile_count, dtype=jnp.int32))
    partial_rank = jnp.einsum(
        "ntd,nedr->nter", tile_slices, fetched, preferred_element_type=jnp.float32
    )
    summed = lax.psum(partial_rank, "expert")
    lowrank = summed.astype(jnp.bfloat16)
    tenant_list = adapter_up_weight.shape[0]
    select_tenant = (
        tile_tenant_index[:, None] == jnp.arange(tenant_list, dtype=jnp.int32)[None, :]
    ).astype(adapter_up_weight.dtype)
    tile_up = jnp.einsum(
        "cj,jvqz->cvqz", select_tenant, adapter_up_weight, preferred_element_type=jnp.float32
    ).astype(jnp.bfloat16)
    adapted_hidden = jnp.einsum(
        "nter,nerf->ntef", lowrank, tile_up, preferred_element_type=jnp.float32
    )
    adapted_hidden = adapted_hidden.reshape(tokens, window, adapted_hidden.shape[3])
    gate_pre = jnp.einsum(
        "td,edf->tef", input_rows, gate_weight, preferred_element_type=jnp.float32
    )
    up_projection_value = (
        jnp.einsum("td,edf->tef", input_rows, up_weight, preferred_element_type=jnp.float32)
        + ADAPTER_SCALE * adapted_hidden
    )
    hidden = (weight[:, :, None] * jax.nn.silu(gate_pre) * up_projection_value).astype(jnp.bfloat16)
    partial_out = jnp.einsum(
        "tef,efd->td",
        lax.all_gather(hidden, "expert", axis=2, tiled=True),
        down_weight,
        preferred_element_type=jnp.float32,
    )
    mixed_rows = lax.psum_scatter(partial_out, "wide", scatter_dimension=0, tiled=True)
    return mixed_rows.astype(jnp.bfloat16)


def solution(mesh):
    in_specs = (
        P(("groups", "wide"), None, "expert"),
        P("groups"),
        P("groups", None),
        P("groups"),
        P("groups"),
        P(),
        P(None, None, ("wide", "expert")),
        P(None, None, ("wide", "expert")),
        P(None, "wide", "expert"),
        P(("groups", "wide"), None, "expert", None),
        P("groups", None, None, ("wide", "expert")),
    )
    out_specs = P(("groups", "wide"), "expert")
    return jax.shard_map(
        per_device, mesh=mesh, in_specs=in_specs, out_specs=out_specs, check_vma=False
    )
```

profile of v0, /device:TPU:0, one launch (start us, length us, event | category | flops | bytes accessed | tf_op | source)
XLA Modules:
  0.0 514.7 jit_solution(17569741497082177469)
XLA Ops:
  6.5 0.7 all-gather.6.cloned.1.call-update
  7.3 1.4 fusion.18
  10.5 38.3 %all-gather.6.cloned.1.call-done = bf16[1,128,6144]{2,1,0:T(8,128)(2,1)} async-done(((bf16[1,128,1536]{2,1,0:T(8,128)(2,1)}), bf16[1,128,6144]{2,1,0:T(8,128)(2,1)}) %all-gather.6.cloned.1.call-update) | async-done | bytes 1572880 | tf_op jit(solution)/shard_map/all_gather | solution.py:31
  48.8 3.7 select_bitcast_fusion
  52.5 0.6 copy-done.10
  53.1 0.6 gather_fusion
  53.8 2.5 fusion.6
  56.3 89.6 %all-reduce.5.cloned.1.call-done = (bf16[128,6144]{1,0:T(8,128)(2,1)}, bf16[128,6144]{1,0:T(8,128)(2,1)}, bf16[128,6144]{1,0:T(8,128)(2,1)}) async-done(((bf16[128,6144]{1,0:T(8,128)(2,1)}, bf16[128,6144]{1,0:T(8,128)(2,1)}, bf16[128,6144]{1,0:T(8,128)(2,1)}), (bf16[128,6144]{1,0:T(8,128)(2,1)}, bf16[128,6144]{1,0:T(8,128)(2,1)}, bf16[128,6144]{1,0:T(8,128)(2,1)})) %all-reduce.5.cloned.1.call-update) | async-done | bytes 4718608 | tf_op jit(solution)/shard_map/psum | solution.py:12
  145.9 1.7 constant_dynamic-update-slice_fusion.3
  147.5 0.2 copy-done.7
  147.8 0.1 constant_dynamic-update-slice_fusion.2
  147.9 0.3 copy-done.6
  148.4 0.4 copy-done.8
  148.8 1.3 fusion.19
  150.3 0.6 copy-done.3
  150.9 134.1 %while.10 = (s32[]{:T(128)}, bf16[3,2,1536,64]{3,2,1,0:T(8,128)(2,1)}, s32[3]{0:T(128)S(1)}, s32[3]{0:T(128)S(1)}, s32[3]{0:T(128)S(1)}, /*index=5*/bf16[2,2,153...) while((s32[]{:T(128)}, ...), condition=%wide.region_6.7_spmd, body=%wide.region_4.6_spmd.sunk | while | flops 393228 | bytes 7078207 | solution.py:62
  150.9 0.6 dynamic_slice.25
  153.4 0.6 dynamic_slice.26
  156.0 0.4 copy.26
  156.4 0.6 dynamic_slice.27
  157.6 1.0 broadcast_select_fusion.2
  158.7 34.9 %all-reduce.7.cloned.1.call-done = bf16[1,2,1536,64]{3,2,1,0:T(8,128)(2,1)} async-done(((bf16[1,2,1536,64]{3,2,1,0:T(8,128)(2,1)}), bf16[1,2,1536,64]{3,2,1,0:T(8,128)(2,1)}) %all-reduce.7.cloned.1.call-update) | async-done | bytes 393232 | tf_op jit(solution)/shard_map/while/body/eval_jaxpr/psum | solution.py:12
  193.6 2.1 constant_dynamic-update-slice_fusion.5
  195.7 0.6 dynamic_slice.25
  198.2 0.6 dynamic_slice.26
  200.8 0.4 copy.26
  201.1 0.6 dynamic_slice.27
  202.4 1.0 broadcast_select_fusion.2
  203.4 34.8 %all-reduce.7.cloned.1.call-done = bf16[1,2,1536,64]{3,2,1,0:T(8,128)(2,1)} async-done(((bf16[1,2,1536,64]{3,2,1,0:T(8,128)(2,1)}), bf16[1,2,1536,64]{3,2,1,0:T(8,128)(2,1)}) %all-reduce.7.cloned.1.call-update) | async-done | bytes 393232 | tf_op jit(solution)/shard_map/while/body/eval_jaxpr/psum | solution.py:12
  238.2 2.1 constant_dynamic-update-slice_fusion.5
  240.3 0.6 dynamic_slice.25
  242.8 0.6 dynamic_slice.26
  245.4 0.4 copy.26
  245.8 0.6 dynamic_slice.27
  247.0 1.0 broadcast_select_fusion.2
  248.1 34.8 %all-reduce.7.cloned.1.call-done = bf16[1,2,1536,64]{3,2,1,0:T(8,128)(2,1)} async-done(((bf16[1,2,1536,64]{3,2,1,0:T(8,128)(2,1)}), bf16[1,2,1536,64]{3,2,1,0:T(8,128)(2,1)}) %all-reduce.7.cloned.1.call-update) | async-done | bytes 393232 | tf_op jit(solution)/shard_map/while/body/eval_jaxpr/psum | solution.py:12
  282.9 2.1 constant_dynamic-update-slice_fusion.5
  285.0 2.6 fusion.20
  287.6 22.5 %all-reduce.8 = bf16[3,128,2,64]{1,3,2,0:T(8,128)(2,1)S(1)} all-reduce(f32[3,128,2,64]{1,3,2,0:T(8,128)S(1)} %fusion.20), channel_id=1, replica_groups=mesh['groups'=2,'wide'=4,'expert'=4] {'expert'}, use_global_device_ids=true, to_apply=%region_7.8 | all-reduce | flops 49152 | bytes 294912 | tf_op jit(solution)/shard_map/psum | solution.py:66
  310.1 0.8 multiply_bitcast_fusion
  310.8 0.2 copy.15
  311.1 1.2 slice-done.1
  312.2 15.1 %fusion.2 = f32[384,2,1024]{2,0,1:T(8,128)} fusion(bf16[2,6144,1024]{2,1,0:T(8,128)(2,1)} %param.19, bf16[384,6144]{1,0:T(8,128)(2,1)S(1)} %bitcast.68), kind=kOutput, calls=%fused_computation.6 | convolution fusion | flops 9663676416 | bytes 33030144 | tf_op jit(solution)/shard_map/td,edf->tef/dot_general | solution.py:79
  327.4 16.2 %fusion.5 = bf16[384,2,1024]{2,0,1:T(8,128)(2,1)} fusion(f32[3,128,2,1024]{3,1,0,2:T(8,128)S(1)} %copy.15, f32[384,2,1024]{2,0,1:T(8,128)} %fusion.2, f32[384,2]{0,1:T(2,128)S(1)} %fusion.13, bf16[2,6144,1024]{2,1,0:T(8,128)(2,1)} %param.20, bf16[384,6144]{1,0:T(8,128)(2,1)S(1)} %bitcast.68), kind=kOutput, calls=%fused_computation.10 | convolution fusion | flops 9669967872 | bytes 37751808 | tf_op jit(solution)/shard_map/td,edf->tef/dot_general | solution.py:83
  343.7 113.3 %all-gather.4.cloned.1.call-done = bf16[384,2,4096]{2,0,1:T(8,128)(2,1)} async-done(((bf16[384,2,1024]{2,0,1:T(8,128)(2,1)}), bf16[384,2,4096]{2,0,1:T(8,128)(2,1)}) %all-gather.4.cloned.1.call-update) | async-done | bytes 6291472 | tf_op jit(solution)/shard_map/all_gather | solution.py:89
  456.9 17.7 %convolution_bitcast_fusion = f32[384,1536]{1,0:T(8,128)} fusion(bf16[384,2,4096]{2,0,1:T(8,128)(2,1)} %all-gather.4.cloned.1.call-done, bf16[2,4096,1536]{2,1,0:T(8,128)(2,1)} %param.21), kind=kOutput, calls=%fused_computation.12 | convolution fusion | flops 9663676416 | bytes 33816576 | tf_op jit(solution)/shard_map/tef,efd->td/dot_general | solution.py:87
  474.6 31.4 %reduce-scatter.2.cloned.1.call-done = f32[96,1536]{1,0:T(8,128)} async-done(((f32[384,1536]{1,0:T(8,128)}), f32[96,1536]{1,0:T(8,128)}) %reduce-scatter.2.cloned.1.call-update) | async-done | bytes 589840 | tf_op jit(solution)/shard_map/reduce_scatter | solution.py:93
  506.0 1.8 convert_element_type.20
  (49 shorter events, 0.7 us)
Async XLA Ops:
  6.5 47.3 %copy-start = (bf16[8,2,64,1024]{3,2,1,0:T(8,128)(2,1)S(1)}, bf16[8,2,64,1024]{3,2,1,0:T(8,128)(2,1)}, u32[]{:S(2)}) copy-start(bf16[8,2,64,1024]{3,2,1,0:T(8,128)(2,1)} %param.23) | copy-start | bytes 6291460
  6.5 42.2 %all-gather.6.cloned.1.call-start = ((), (), s32[]{:S(2)}) async-start(), calls=%async_computation.3 | async-start | bytes 1966080 | tf_op jit(solution)/shard_map/all_gather | solution.py:31
  7.3 138.6 %all-reduce.5.cloned.1.call-start = ((), (), s32[]{:S(2)}) async-start(), calls=%async_computation.4 | async-start | bytes 9437184 | tf_op jit(solution)/shard_map/psum | solution.py:12
  52.4 0.7 copy-start.10
  52.4 0.7 copy-start.2
  52.4 1.3 copy-start.9
  145.9 1.9 copy-start.7
  145.9 2.4 copy-start.6
  147.8 1.0 copy-start.8
  148.8 2.1 copy-start.3
  148.8 2.1 copy-start.4
  150.9 42.7 %all-reduce.7.cloned.1.call-start = ((), (), s32[]{:S(2)}) async-start(), calls=%async_computation.5 | async-start | bytes 1572864 | tf_op jit(solution)/shard_map/while/body/eval_jaxpr/psum | solution.py:12
  195.7 42.6 %all-reduce.7.cloned.1.call-start = ((), (), s32[]{:S(2)}) async-start(), calls=%async_computation.5 | async-start | bytes 1572864 | tf_op jit(solution)/shard_map/while/body/eval_jaxpr/psum | solution.py:12
  240.3 42.6 %all-reduce.7.cloned.1.call-start = ((), (), s32[]{:S(2)}) async-start(), calls=%async_computation.5 | async-start | bytes 1572864 | tf_op jit(solution)/shard_map/while/body/eval_jaxpr/psum | solution.py:12
  285.0 25.1 %copy-start.5 = (bf16[3,2,64,1024]{3,0,2,1:T(4,128)(2,1)S(1)}, bf16[3,2,64,1024]{3,0,2,1:T(4,128)(2,1)}, u32[]{:S(2)}) copy-start(bf16[3,2,64,1024]{3,0,2,1:T(4,128)(2,1)} %fusion.6) | copy-start | bytes 2359300
  285.0 171.9 %all-gather.4.cloned.1.call-start = ((), (), s32[]{:S(2)}) async-start(), calls=%async_computation.1 | async-start | bytes 7864320 | tf_op jit(solution)/shard_map/all_gather | solution.py:89
  285.0 26.1 %slice-start = ((s8[4718592]{0:T(1024)(128)(4,1)}), s8[524288]{0:T(1024)(128)(4,1)S(1)}, s32[]{:S(2)}) async-start(s8[4718592]{0:T(1024)(128)(4,1)} %bitcast.67), calls=%async_computation.6 | async-start | bytes 1048576
  310.1 2.2 slice-start.1
  343.6 162.4 %reduce-scatter.2.cloned.1.call-start = ((), (), s32[]{:S(2)}) async-start(), calls=%async_computation.2 | async-start | bytes 2949120 | tf_op jit(solution)/shard_map/reduce_scatter | solution.py:93
  456.9 50.9 %copy-start.1 = (bf16[8,2,64,1024]{3,2,1,0:T(8,128)(2,1)S(1)}, bf16[8,2,64,1024]{3,2,1,0:T(8,128)(2,1)}, u32[]{:S(2)}) copy-start(bf16[8,2,64,1024]{3,2,1,0:T(8,128)(2,1)} %param.23) | copy-start | bytes 6291460
Sparse Core Ops, SparseCore 0:
  8.9 39.7 all-gather.5
  52.6 93.2 all-reduce.4
  158.8 34.7 all-reduce.6
  203.5 34.6 all-reduce.6
  248.2 34.6 all-reduce.6
  343.7 113.1 all-gather.3
  474.7 31.2 reduce-scatter.1
where the time goes:
time: 515 us
  waiting for transfers between devices  378 us (73%)
  matrix products  56.1 us (11%)
  blocking collectives  22.5 us (4%)
  local copies, waits for them, and re-layouts  20.4 us (4%)
  between operations  15.4 us (3%)
  loops' own time  13.7 us (3%)
  other arithmetic  8.61 us (2%)
    psum x4, waiting for transfers between devices, spread(): return lax.psum(block, axis)  194 us
    all_gather x1, waiting for transfers between devices, per_device(): lax.all_gather(hidden, 'expert', axis=2, tiled=True)  113 us
    all_gather x1, waiting for transfers between devices, per_device(): full_slot = lax.all_gather(own_slot, 'expert', axis=1, tiled=True)  38.3 us
    reduce_scatter x1, waiting for transfers between devices, per_device(): lax.psum_scatter(partial_out, 'wide', scatter_dimension=0, tiled=True)  31.4 us
    psum x1, blocking collectives, per_device(): summed = lax.psum(partial_rank, 'expert')  22.5 us
    dot_general x1, matrix products, per_device(): jnp.einsum('tef,efd->td', lax.all_gather(hidden, 'expert', axis=2, tiled=...  17.7 us
    dot_general x1, matrix products, per_device(): jnp.einsum('td,edf->tef', input_rows, up_weight, preferred_element_type=j...  16.2 us
    dot_general x1, matrix products, per_device(): jnp.einsum('td,edf->tef', input_rows, gate_weight, preferred_element_type...  15.1 us
  transfers between devices with their start and end apart: 7, of which 7 were waited for; matrix products, arithmetic and copies ran while one was open for 1% of the time, Pallas kernels for 0%

commit v1 on v0

--- a/solution.py
+++ b/solution.py
@@ -84,12 +84,38 @@
         + ADAPTER_SCALE * adapted_hidden
     )
     hidden = (weight[:, :, None] * jax.nn.silu(gate_pre) * up_projection_value).astype(jnp.bfloat16)
-    partial_out = jnp.einsum(
+    size, index, span = (lax.axis_size("expert"), lax.axis_index("expert"), hidden.shape[2])
+    right = [(i, (i + 1) % size) for i in range(size)]
+    left = [(i, (i - 1) % size) for i in range(size)]
+    half = size // 2
+    from_left = from_right = hidden
+    so_far = jnp.einsum(
         "tef,efd->td",
-        lax.all_gather(hidden, "expert", axis=2, tiled=True),
-        down_weight,
+        hidden,
+        lax.dynamic_slice_in_dim(down_weight, index * span, hidden.shape[2], axis=1),
         preferred_element_type=jnp.float32,
     )
+    for hop in range(1, half + 1):
+        from_left = lax.ppermute(from_left, "expert", right)
+        if hop < size - half:
+            from_right = lax.ppermute(from_right, "expert", left)
+            so_far = so_far + jnp.einsum(
+                "tef,efd->td",
+                from_right,
+                lax.dynamic_slice_in_dim(
+                    down_weight, (index + hop) % size * span, from_right.shape[2], axis=1
+                ),
+                preferred_element_type=jnp.float32,
+            )
+        so_far = so_far + jnp.einsum(
+            "tef,efd->td",
+            from_left,
+            lax.dynamic_slice_in_dim(
+                down_weight, (index - hop) % size * span, from_left.shape[2], axis=1
+            ),
+            preferred_element_type=jnp.float32,
+        )
+    partial_out = so_far
     mixed_rows = lax.psum_scatter(partial_out, "wide", scatter_dimension=0, tiled=True)
     return mixed_rows.astype(jnp.bfloat16)
 

time: 515 us -> 492 us (0.955)
  waiting for transfers between devices: 378 us -> 319 us
  starting transfers between devices: 0.09 us -> 30.6 us
    all_gather x1 -> x0, waiting for transfers between devices: 113 us -> none  [per_device(): lax.all_gather(hidden, 'expert', axis=2, tiled=True)]
    ppermute x0 -> x3, waiting for transfers between devices: none -> 55.5 us  [the longest x2 55.5 us: per_device(): from_left = lax.ppermute(from_left, 'expert', right)]
    ppermute x0 -> x3, starting transfers between devices: none -> 30.6 us  [the longest x2 26.8 us: per_device(): from_left = lax.ppermute(from_left, 'expert', right)]
    dot_general x1 -> x4, matrix products: 17.7 us -> 21.7 us  [the longest x2 11.8 us: per_device(): jnp.einsum('tef,efd->td', from_left, lax.dynamic_slice_in_dim(down_weight...]
  transfers between devices with their start and end apart: 7 -> 9, of which waited for: 7 -> 8; matrix products, arithmetic and copies ran while one was open for 1% -> 4% of each run, Pallas kernels for 0% -> 0%
where the time goes in v1:
time: 492 us; the launch traced here: 491 us
  waiting for transfers between devices  319 us (65%)
  matrix products  59.2 us (12%)
  starting transfers between devices  30.6 us (6%)
  blocking collectives  22.5 us (5%)
  local copies, waits for them, and re-layouts  21.3 us (4%)
  between operations  15.5 us (3%)
  loops' own time  13.7 us (3%)
  other arithmetic  8.61 us (2%)
    psum x4, waiting for transfers between devices, spread(): return lax.psum(block, axis)  194 us
    ppermute x2, waiting for transfers between devices, per_device(): from_left = lax.ppermute(from_left, 'expert', right)  55.5 us
    all_gather x1, waiting for transfers between devices, per_device(): full_slot = lax.all_gather(own_slot, 'expert', axis=1, tiled=True)  38.3 us
    reduce_scatter x1, waiting for transfers between devices, per_device(): lax.psum_scatter(partial_out, 'wide', scatter_dimension=0, tiled=True)  30.8 us
    ppermute x2, starting transfers between devices, per_device(): from_left = lax.ppermute(from_left, 'expert', right)  26.8 us
    psum x1, blocking collectives, per_device(): summed = lax.psum(partial_rank, 'expert')  22.5 us
    dot_general x1, matrix products, per_device(): jnp.einsum('td,edf->tef', input_rows, up_weight, preferred_element_type=j...  15.3 us
    dot_general x1, matrix products, per_device(): jnp.einsum('td,edf->tef', input_rows, gate_weight, preferred_element_type...  15.1 us
  transfers between devices with their start and end apart: 9, of which 8 were waited for; matrix products, arithmetic and copies ran while one was open for 4% of the time, Pallas kernels for 0%

profile of v1, /device:TPU:0, one launch (start us, length us, event | category | flops | bytes accessed | tf_op | source)
XLA Modules:
  0.0 490.9 jit_solution(393987715352088893)
XLA Ops:
  6.5 0.7 all-gather.3.cloned.1.call-update
  7.3 1.4 fusion.51
  10.5 38.3 %all-gather.3.cloned.1.call-done = bf16[1,128,6144]{2,1,0:T(8,128)(2,1)} async-done(((bf16[1,128,1536]{2,1,0:T(8,128)(2,1)}), bf16[1,128,6144]{2,1,0:T(8,128)(2,1)}) %all-gather.3.cloned.1.call-update) | async-done | bytes 1572880 | tf_op jit(solution)/shard_map/all_gather | solution.py:31
  48.8 3.7 select_bitcast_fusion
  52.5 0.6 copy-done.10
  53.1 0.6 gather_fusion
  53.8 2.5 fusion.35
  56.3 89.6 %all-reduce.5.cloned.1.call-done = (bf16[128,6144]{1,0:T(8,128)(2,1)}, bf16[128,6144]{1,0:T(8,128)(2,1)}, bf16[128,6144]{1,0:T(8,128)(2,1)}) async-done(((bf16[128,6144]{1,0:T(8,128)(2,1)}, bf16[128,6144]{1,0:T(8,128)(2,1)}, bf16[128,6144]{1,0:T(8,128)(2,1)}), (bf16[128,6144]{1,0:T(8,128)(2,1)}, bf16[128,6144]{1,0:T(8,128)(2,1)}, bf16[128,6144]{1,0:T(8,128)(2,1)})) %all-reduce.5.cloned.1.call-update) | async-done | bytes 4718608 | tf_op jit(solution)/shard_map/psum | solution.py:12
  145.9 1.6 constant_dynamic-update-slice_fusion.3
  147.9 1.1 copy-done.6
  149.1 1.3 fusion.52
  150.5 0.7 copy-done.3
  151.4 0.5 copy-done.4
  151.9 134.1 %while.10 = (s32[]{:T(128)}, bf16[3,2,1536,64]{3,2,1,0:T(8,128)(2,1)}, s32[3]{0:T(128)S(1)}, s32[3]{0:T(128)S(1)}, s32[3]{0:T(128)S(1)}, /*index=5*/bf16[2,2,153...) while((s32[]{:T(128)}, ...), condition=%wide.region_6.7_spmd, body=%wide.region_4.6_spmd.sunk | while | flops 393228 | bytes 7078207 | solution.py:62
  151.9 0.6 dynamic_slice.63
  154.4 0.6 dynamic_slice.64
  157.3 0.6 dynamic_slice.65
  158.6 1.0 broadcast_select_fusion.2
  159.6 34.9 %all-reduce.7.cloned.1.call-done = bf16[1,2,1536,64]{3,2,1,0:T(8,128)(2,1)} async-done(((bf16[1,2,1536,64]{3,2,1,0:T(8,128)(2,1)}), bf16[1,2,1536,64]{3,2,1,0:T(8,128)(2,1)}) %all-reduce.7.cloned.1.call-update) | async-done | bytes 393232 | tf_op jit(solution)/shard_map/while/body/eval_jaxpr/psum | solution.py:12
  194.5 2.1 constant_dynamic-update-slice_fusion.5
  196.6 0.6 dynamic_slice.63
  199.1 0.6 dynamic_slice.64
  202.1 0.6 dynamic_slice.65
  203.3 1.0 broadcast_select_fusion.2
  204.4 34.8 %all-reduce.7.cloned.1.call-done = bf16[1,2,1536,64]{3,2,1,0:T(8,128)(2,1)} async-done(((bf16[1,2,1536,64]{3,2,1,0:T(8,128)(2,1)}), bf16[1,2,1536,64]{3,2,1,0:T(8,128)(2,1)}) %all-reduce.7.cloned.1.call-update) | async-done | bytes 393232 | tf_op jit(solution)/shard_map/while/body/eval_jaxpr/psum | solution.py:12
  239.2 2.1 constant_dynamic-update-slice_fusion.5
  241.3 0.6 dynamic_slice.63
  243.8 0.6 dynamic_slice.64
  246.7 0.6 dynamic_slice.65
  248.0 1.0 broadcast_select_fusion.2
  249.0 34.8 %all-reduce.7.cloned.1.call-done = bf16[1,2,1536,64]{3,2,1,0:T(8,128)(2,1)} async-done(((bf16[1,2,1536,64]{3,2,1,0:T(8,128)(2,1)}), bf16[1,2,1536,64]{3,2,1,0:T(8,128)(2,1)}) %all-reduce.7.cloned.1.call-update) | async-done | bytes 393232 | tf_op jit(solution)/shard_map/while/body/eval_jaxpr/psum | solution.py:12
  283.8 2.1 constant_dynamic-update-slice_fusion.5
  285.9 2.6 fusion.53
  288.5 22.5 %all-reduce.8 = bf16[3,128,2,64]{1,3,2,0:T(8,128)(2,1)S(1)} all-reduce(f32[3,128,2,64]{1,3,2,0:T(8,128)S(1)} %fusion.53), channel_id=1, replica_groups=mesh['groups'=2,'wide'=4,'expert'=4] {'expert'}, use_global_device_ids=true, to_apply=%region_7.8 | all-reduce | flops 49152 | bytes 294912 | tf_op jit(solution)/shard_map/psum | solution.py:66
  311.0 0.8 multiply_bitcast_fusion
  312.0 1.2 slice-done.1
  313.2 15.1 %fusion.10 = f32[384,2,1024]{2,0,1:T(8,128)} fusion(bf16[2,6144,1024]{2,1,0:T(8,128)(2,1)} %param.19, bf16[384,6144]{1,0:T(8,128)(2,1)S(1)} %bitcast.82), kind=kOutput, calls=%fused_computation.14 | convolution fusion | flops 9663676416 | bytes 33030144 | tf_op jit(solution)/shard_map/td,edf->tef/dot_general | solution.py:79
  328.3 15.3 %fusion.13 = bf16[384,2,1024]{2,0,1:T(8,128)(2,1)S(1)} fusion(f32[3,128,2,1024]{3,1,0,2:T(8,128)S(1)} %copy.15, f32[384,2,1024]{2,0,1:T(8,128)} %fusion.10, f32[384,2]{0,1:T(2,128)S(1)} %fusion.42, bf16[2,6144,1024]{2,1,0:T(8,128)(2,1)} %param.20, bf16[384,6144]{1,0:T(8,128)(2,1)S(1)} %bitcast.82), kind=kOutput, calls=%fused_computation.18 | convolution fusion | flops 9669967872 | bytes 37751808 | tf_op jit(solution)/shard_map/td,edf->tef/dot_general | solution.py:83
  343.7 3.8 collective-permute-start
  347.5 35.3 %collective-permute-done.1 = bf16[384,2,1024]{2,0,1:T(8,128)(2,1)S(1)} collective-permute-done((bf16[384,2,1024]{2,0,1:T(8,128)(2,1)S(1)}, bf16[384,2,1024]{2,0,1:T(8,128)(2,1)S(1)}, u32[]{:S(2)}, u32[]{:S(2)}) %collective-permute-start.1) | collective-permute-done | bytes 1572896 | tf_op jit(solution)/shard_map/ppermute | solution.py:99
  382.8 26.7 %collective-permute-start.2 = (bf16[384,2,1024]{2,0,1:T(8,128)(2,1)S(1)}, bf16[384,2,1024]{2,0,1:T(8,128)(2,1)S(1)}, u32[]{:S(2)}, u32[]{:S(2)}) collective-permute-start(bf16[384,2,1024]{2,0,1:T(8,128)(2,1)S(1)} %collective-permute-done.1), channel_id=1, source_target_pairs={{0,1},{1,2},{2,3},{3,0},{4,5},{5,6},{6,7},{7,4},{8,9},{9,10},{10,1... | collective-permute-start | bytes 4718600 | tf_op jit(solution)/shard_map/ppermute | solution.py:99
  409.5 4.7 fusion.14
  414.3 5.2 %fusion.32 = f32[384,1536]{1,0:T(8,128)S(1)} fusion(f32[384,1536]{1,0:T(8,128)S(1)} %fusion.14, bf16[384,2,1024]{2,0,1:T(8,128)(2,1)} %collective-permute-done, bf16[2,4096,1536]{2,1,0:T(8,128)(2,1)} %param.21, s32[]{:T(128)S(6)} %select_n.101), kind=kOutput, calls=%fused_computation.26 | convolution fusion | flops 2416508928 | bytes 12582916 | tf_op jit(solution)/shard_map/tef,efd->td/dot_general | solution.py:102
  419.5 4.7 fusion.29
  424.2 20.2 %collective-permute-done.2 = bf16[384,2,1024]{2,0,1:T(8,128)(2,1)S(1)} collective-permute-done((bf16[384,2,1024]{2,0,1:T(8,128)(2,1)S(1)}, bf16[384,2,1024]{2,0,1:T(8,128)(2,1)S(1)}, u32[]{:S(2)}, u32[]{:S(2)}) %collective-permute-start.2) | collective-permute-done | bytes 1572896 | tf_op jit(solution)/shard_map/ppermute | solution.py:99
  444.5 7.0 %fusion.26 = f32[384,1536]{1,0:T(8,128)} fusion(f32[384,1536]{1,0:T(8,128)S(1)} %fusion.29, bf16[384,2,1024]{2,0,1:T(8,128)(2,1)S(1)} %collective-permute-done.2, bf16[2,4096,1536]{2,1,0:T(8,128)(2,1)} %param.21, s32[]{:T(128)S(6)} %select_n.105), kind=kOutput, calls=%fused_computation.24 | convolution fusion | flops 2416508928 | bytes 12582916 | tf_op jit(solution)/shard_map/tef,efd->td/dot_general | solution.py:110
  451.5 30.8 %reduce-scatter.2.cloned.1.call-done = f32[96,1536]{1,0:T(8,128)} async-done(((f32[384,1536]{1,0:T(8,128)}), f32[96,1536]{1,0:T(8,128)}) %reduce-scatter.2.cloned.1.call-update) | async-done | bytes 589840 | tf_op jit(solution)/shard_map/reduce_scatter | solution.py:119
  482.3 1.8 convert_element_type.20
  (55 shorter events, 2.4 us)
Async XLA Ops:
  6.5 47.3 %copy-start = (bf16[8,2,64,1024]{3,2,1,0:T(8,128)(2,1)S(1)}, bf16[8,2,64,1024]{3,2,1,0:T(8,128)(2,1)}, u32[]{:S(2)}) copy-start(bf16[8,2,64,1024]{3,2,1,0:T(8,128)(2,1)} %param.23) | copy-start | bytes 6291460
  6.5 42.2 %all-gather.3.cloned.1.call-start = ((), (), s32[]{:S(2)}) async-start(), calls=%async_computation.2 | async-start | bytes 1966080 | tf_op jit(solution)/shard_map/all_gather | solution.py:31
  7.3 138.6 %all-reduce.5.cloned.1.call-start = ((), (), s32[]{:S(2)}) async-start(), calls=%async_computation.3 | async-start | bytes 9437184 | tf_op jit(solution)/shard_map/psum | solution.py:12
  52.4 0.7 copy-start.10
  52.4 0.7 copy-start.2
  52.4 1.3 copy-start.9
  145.9 1.9 copy-start.7
  147.5 1.5 copy-start.6
  147.9 1.2 copy-start.8
  149.1 2.1 copy-start.3
  150.5 1.4 copy-start.4
  151.9 42.7 %all-reduce.7.cloned.1.call-start = ((), (), s32[]{:S(2)}) async-start(), calls=%async_computation.4 | async-start | bytes 1572864 | tf_op jit(solution)/shard_map/while/body/eval_jaxpr/psum | solution.py:12
  196.6 42.6 %all-reduce.7.cloned.1.call-start = ((), (), s32[]{:S(2)}) async-start(), calls=%async_computation.4 | async-start | bytes 1572864 | tf_op jit(solution)/shard_map/while/body/eval_jaxpr/psum | solution.py:12
  241.3 42.6 %all-reduce.7.cloned.1.call-start = ((), (), s32[]{:S(2)}) async-start(), calls=%async_computation.4 | async-start | bytes 1572864 | tf_op jit(solution)/shard_map/while/body/eval_jaxpr/psum | solution.py:12
  285.9 25.1 %copy-start.5 = (bf16[3,2,64,1024]{3,0,2,1:T(4,128)(2,1)S(1)}, bf16[3,2,64,1024]{3,0,2,1:T(4,128)(2,1)}, u32[]{:S(2)}) copy-start(bf16[3,2,64,1024]{3,0,2,1:T(4,128)(2,1)} %fusion.35) | copy-start | bytes 2359300
  285.9 196.3 %reduce-scatter.2.cloned.1.call-start = ((), (), s32[]{:S(2)}) async-start(), calls=%async_computation.1 | async-start | bytes 2949120 | tf_op jit(solution)/shard_map/reduce_scatter | solution.py:119
  285.9 26.1 %slice-start = ((s8[4718592]{0:T(1024)(128)(4,1)}), s8[524288]{0:T(1024)(128)(4,1)S(1)}, s32[]{:S(2)}) async-start(s8[4718592]{0:T(1024)(128)(4,1)} %bitcast.81), calls=%async_computation.5 | async-start | bytes 1048576
  311.0 2.2 slice-start.1
  343.7 39.2 %collective-permute-start.1 = (bf16[384,2,1024]{2,0,1:T(8,128)(2,1)S(1)}, bf16[384,2,1024]{2,0,1:T(8,128)(2,1)S(1)}, u32[]{:S(2)}, u32[]{:S(2)}) collective-permute-start(bf16[384,2,1024]{2,0,1:T(8,128)(2,1)S(1)} %fusion.13), channel_id=1, source_target_pairs={{0,1},{1,2},{2,3},{3,0},{4,5},{5,6},{6,7},{7,4},{8,9},{9,10},{10,1... | collective-permute-start | bytes 4718600 | tf_op jit(solution)/shard_map/ppermute | solution.py:99
  343.7 70.5 %collective-permute-start = (bf16[384,2,1024]{2,0,1:T(8,128)(2,1)S(1)}, bf16[384,2,1024]{2,0,1:T(8,128)(2,1)}, u32[]{:S(2)}, u32[]{:S(2)}) collective-permute-start(bf16[384,2,1024]{2,0,1:T(8,128)(2,1)S(1)} %fusion.13), channel_id=1, source_target_pairs={{0,3},{1,0},{2,1},{3,2},{4,7},{5,4},{6,5},{7,6},{8,11},{9,8},{10,9... | collective-permute-start | bytes 4718600 | tf_op jit(solution)/shard_map/ppermute | solution.py:101
  382.8 61.6 %collective-permute-start.2 = (bf16[384,2,1024]{2,0,1:T(8,128)(2,1)S(1)}, bf16[384,2,1024]{2,0,1:T(8,128)(2,1)S(1)}, u32[]{:S(2)}, u32[]{:S(2)}) collective-permute-start(bf16[384,2,1024]{2,0,1:T(8,128)(2,1)S(1)} %collective-permute-done.1), channel_id=1, source_target_pairs={{0,1},{1,2},{2,3},{3,0},{4,5},{5,6},{6,7},{7,4},{8,9},{9,10},{10,1... | collective-permute-start | bytes 4718600 | tf_op jit(solution)/shard_map/ppermute | solution.py:99
  444.5 39.6 %copy-start.1 = (bf16[8,2,64,1024]{3,2,1,0:T(8,128)(2,1)S(1)}, bf16[8,2,64,1024]{3,2,1,0:T(8,128)(2,1)}, u32[]{:S(2)}) copy-start(bf16[8,2,64,1024]{3,2,1,0:T(8,128)(2,1)} %param.23) | copy-start | bytes 6291460
Sparse Core Ops, SparseCore 0:
  8.9 39.7 all-gather.2
  52.6 93.2 all-reduce.4
  159.7 34.7 all-reduce.6
  204.5 34.6 all-reduce.6
  249.1 34.6 all-reduce.6
  451.6 30.6 reduce-scatter.1
